TPU v7x, 512 devices: a whole 4x8x8 slice. The times are simulated.
512 devices in a mesh: seq: 128 (over z, y_hi, x, core), head: 4 (over y_lo).
Axes of the slice: x: 4, y: 8 (y_hi: 2, y_lo: 4; y = y_hi * 4 + y_lo), z: 8, core: 2. Of those that a mesh axis runs over, the one named last changes fastest.
Arguments:
- query_rows: bfloat16 [32768, 8, 128], P('seq', 'head'), may hold values from -20 to 20
- key_rows: bfloat16 [32768, 8, 128], P('seq', 'head'), may hold values from -20 to 20
- value_rows: bfloat16 [32768, 8, 128], P('seq', 'head'), may hold values from -6 to 6
- cotangent: bfloat16 [32768, 8, 128], P('seq', 'head'), may hold values from -6 to 6
- norm_gain: float32 [8, 128], P('head'), may hold values from 0.5 to 2
- offsets: int32 [8], P('head'), may hold values from 0 to 31, as said below
Outputs:
- query_grad: bfloat16 [32768, 8, 128], P('seq', 'head')
- key_grad: bfloat16 [32768, 8, 128], P('seq', 'head')
- value_grad: bfloat16 [32768, 8, 128], P('seq', 'head')
Inputs may be any that keep to these rules, and one draw needn't show every extreme that they name: The heads' offsets are distinct.
All inputs are finite; a program needn't handle non-finite values.
Results may differ from a plain program's by a relative error of at most 0.018.
Values may be sent and summed in bfloat16 or wider, within the bound.
No kernel may reach another device: no remote copies, remote signals or barrier semaphores. Data moves between devices by JAX's collectives and lax.ppermute only.
A program may use at most 128 MiB of HBM per device.

v0:
```python
import numpy as np
import jax
import jax.numpy as jnp
from jax import lax
from jax.sharding import Mesh
from jax.sharding import PartitionSpec as P

RATE2 = 4
RATE3 = 16
RATE4 = 32
RATES = (1, RATE2, RATE3, RATE4)
neg_fill = -1e30
epsilon = 1e-05


def pick_rows(source, wanted, stride):
    row_count = source.shape[0] // stride
    shaped = source.reshape((row_count, stride) + source.shape[1:])
    trailing = (1,) * (source.ndim - 2)
    target = wanted.reshape((1, 1, -1) + trailing)
    column = jnp.arange(stride, dtype=jnp.int32).reshape((1, stride, 1) + trailing)
    zeroed = jnp.where(column == target, shaped, jnp.zeros((), source.dtype))
    return jnp.sum(zeroed, axis=1, dtype=source.dtype)


def put_rows(compact, wanted, stride, filler):
    trailing = (1,) * (compact.ndim - 2)
    target = wanted.reshape((1, 1, -1) + trailing)
    column = jnp.arange(stride, dtype=jnp.int32).reshape((1, stride, 1) + trailing)
    spread = jnp.where(column == target, compact[:, None], jnp.asarray(filler, compact.dtype))
    return spread.reshape((compact.shape[0] * stride,) + compact.shape[1:])


def level_plan(tok_dev, seq_count):
    group_rows = tok_dev * seq_count // RATE4
    spans = [max(1, stride * group_rows // tok_dev) for stride in RATES]
    factors = []
    covered = 1
    for span in spans:
        factors.append(span // covered)
        covered = span
    names = tuple(("s%d" % (index + 1) for index in range(len(spans))))
    return (spans, factors, names)


def shards(plan, query_rows, key_rows, value_rows, cotangent, norm_gain, offsets):
    spans, factors, names = plan
    tok_dev, heads_dev, head_size = query_rows.shape
    score_scale = head_size ** (-0.5)
    features = heads_dev * head_size * lax.axis_size("head")
    seq_axes = tuple(reversed(names))
    device = lax.axis_index(seq_axes)
    levels = []
    for index, stride in enumerate(RATES):
        axes = tuple(reversed(names[: index + 1]))
        span = spans[index]
        rows = tok_dev // stride
        wanted = offsets % stride
        place = device % span * rows
        key_sel = pick_rows(key_rows, wanted, stride)
        value_sel = pick_rows(value_rows, wanted, stride)
        query_sel = pick_rows(query_rows, wanted, stride)
        packed = jnp.stack([key_sel, value_sel, query_sel], axis=1)
        gathered = lax.all_gather(packed, axes, axis=0, tiled=True)
        levels.append(
            dict(
                stride=stride,
                axes=axes,
                rows=rows,
                wanted=wanted,
                place=place,
                key_sel=key_sel,
                value_sel=value_sel,
                query_sel=query_sel,
                key_all=gathered[:, 0],
                value_all=gathered[:, 1],
                query_all=gathered[:, 2],
            )
        )
    lse_total = jnp.full((tok_dev, heads_dev), neg_fill, jnp.float32)
    for level in levels:
        total_rows = level["key_all"].shape[0]
        raw = (
            jnp.einsum(
                "qhd,khd->hqk",
                level["query_sel"],
                level["key_all"],
                preferred_element_type=jnp.float32,
            )
            * score_scale
        )
        query_at = level["place"] + jnp.arange(level["rows"], dtype=jnp.int32)
        key_at = jnp.arange(total_rows, dtype=jnp.int32)
        linked = key_at[None, :] <= query_at[:, None]
        scores = jnp.where(linked[None], raw, neg_fill)
        row_peak = jnp.max(scores, axis=2)
        level_lse = row_peak + jnp.log(jnp.sum(jnp.exp(scores - row_peak[:, :, None]), axis=2))
        level["scores"] = scores
        lse_total = jnp.logaddexp(
            lse_total, put_rows(level_lse.T, level["wanted"], level["stride"], neg_fill)
        )
    attended = jnp.zeros((tok_dev, heads_dev, head_size), jnp.float32)
    for level in levels:
        lse_sel = pick_rows(lse_total, level["wanted"], level["stride"])
        weights = jnp.exp(level["scores"] - lse_sel.T[:, :, None])
        level["lse_sel"] = lse_sel
        level["weights"] = weights
        out_sel = jnp.einsum(
            "hqk,khd->qhd",
            weights.astype(jnp.bfloat16),
            level["value_all"],
            preferred_element_type=jnp.float32,
        )
        attended = attended + put_rows(out_sel, level["wanted"], level["stride"], 0.0)
    grad_in = cotangent.astype(jnp.float32) * norm_gain[None]
    sums = lax.psum(
        jnp.stack(
            [
                jnp.sum(attended, axis=(1, 2)),
                jnp.sum(attended * attended, axis=(1, 2)),
                jnp.sum(grad_in, axis=(1, 2)),
                jnp.sum(grad_in * attended, axis=(1, 2)),
            ]
        ),
        "head",
    )
    centre = sums[0] / features
    variance = sums[1] / features - centre * centre
    inverse = lax.rsqrt(variance + epsilon)
    first_mean = sums[2] / features
    second_mean = inverse * (sums[3] / features - centre * first_mean)
    normed = (attended - centre[:, None, None]) * inverse[:, None, None]
    d_attended = (
        inverse[:, None, None]
        * (grad_in - first_mean[:, None, None] - normed * second_mean[:, None, None])
    ).astype(jnp.bfloat16)
    row_delta = jnp.sum(d_attended.astype(jnp.float32) * attended, axis=2)
    query_grad = jnp.zeros((tok_dev, heads_dev, head_size), jnp.float32)
    for level in levels:
        dout_sel = pick_rows(d_attended, level["wanted"], level["stride"])
        delta_sel = pick_rows(row_delta, level["wanted"], level["stride"])
        weight_grad = jnp.einsum(
            "qhd,khd->hqk", dout_sel, level["value_all"], preferred_element_type=jnp.float32
        )
        score_grad = (level["weights"] * (weight_grad - delta_sel.T[:, :, None])).astype(
            jnp.bfloat16
        )
        grad_sel = jnp.einsum(
            "hqk,khd->qhd", score_grad, level["key_all"], preferred_element_type=jnp.float32
        )
        query_grad = query_grad + put_rows(
            grad_sel * score_scale, level["wanted"], level["stride"], 0.0
        )
        level["dout_all"] = lax.all_gather(dout_sel, level["axes"], axis=0, tiled=True)
        stats = jnp.stack([level["lse_sel"], delta_sel], axis=1)
        level["stats_all"] = lax.all_gather(stats, level["axes"], axis=0, tiled=True)
    key_grad = jnp.zeros((tok_dev, heads_dev, head_size), jnp.float32)
    value_grad = jnp.zeros((tok_dev, heads_dev, head_size), jnp.float32)
    for level in levels:
        query_all = level["query_all"]
        dout_all = level["dout_all"]
        lse_all = level["stats_all"][:, 0]
        delta_all = level["stats_all"][:, 1]
        total_rows = query_all.shape[0]
        raw = (
            jnp.einsum(
                "qhd,khd->hqk", query_all, level["key_sel"], preferred_element_type=jnp.float32
            )
            * score_scale
        )
        key_at = level["place"] + jnp.arange(level["rows"], dtype=jnp.int32)
        query_at = jnp.arange(total_rows, dtype=jnp.int32)
        linked = key_at[None, :] <= query_at[:, None]
        scores = jnp.where(linked[None], raw, neg_fill)
        weights = jnp.exp(scores - lse_all.T[:, :, None])
        value_grad_sel = jnp.einsum(
            "hqk,qhd->khd",
            weights.astype(jnp.bfloat16),
            dout_all,
            preferred_element_type=jnp.float32,
        )
        weight_grad = jnp.einsum(
            "qhd,khd->hqk", dout_all, level["value_sel"], preferred_element_type=jnp.float32
        )
        score_grad = (weights * (weight_grad - delta_all.T[:, :, None])).astype(jnp.bfloat16)
        key_grad_sel = jnp.einsum(
            "hqk,qhd->khd", score_grad, query_all, preferred_element_type=jnp.float32
        )
        key_grad = key_grad + put_rows(
            key_grad_sel * score_scale, level["wanted"], level["stride"], 0.0
        )
        value_grad = value_grad + put_rows(value_grad_sel, level["wanted"], level["stride"], 0.0)
    return (
        query_grad.astype(jnp.bfloat16),
        key_grad.astype(jnp.bfloat16),
        value_grad.astype(jnp.bfloat16),
    )


def solution(mesh):
    seq_count = mesh.shape["seq"]
    head_count = mesh.shape["head"]

    def run(query_rows, key_rows, value_rows, cotangent, norm_gain, offsets):
        tok_dev = query_rows.shape[0] // seq_count
        plan = level_plan(tok_dev, seq_count)
        spans, factors, names = plan
        grid = np.asarray(mesh.devices).reshape(tuple(reversed(factors)) + (head_count,))
        sub_mesh = Mesh(grid, tuple(reversed(names)) + ("head",))
        seq_spec = tuple(reversed(names))
        rows_spec = P(seq_spec, "head", None)
        placed = (rows_spec, rows_spec, rows_spec, rows_spec, P("head", None), P("head"))

        def body(*args):
            return shards(plan, *args)

        return jax.shard_map(
            body,
            mesh=sub_mesh,
            in_specs=placed,
            out_specs=(rows_spec, rows_spec, rows_spec),
            check_vma=False,
        )(query_rows, key_rows, value_rows, cotangent, norm_gain, offsets)

    return run
```

profile of v0, /device:TPU:9, one launch (start us, length us, event | category | flops | bytes accessed | tf_op | source)
XLA Modules:
  0.0 1188.4 jit_solution(1432584091598694713)
XLA Ops:
  7.3 1.0 copy.162
  8.3 1.0 fusion.120
  18.5 26.9 %all-gather.5.cloned.1.call-done = bf16[1024,3,2,128]{3,0,2,1:T(8,128)(2,1)} async-done(((bf16[256,3,2,128]{3,0,2,1:T(8,128)(2,1)}), bf16[1024,3,2,128]{3,0,2,1:T(8,128)(2,1)}) %all-gather.5.cloned.1.call-update) | async-done | bytes 1572880 | tf_op jit(solution)/shard_map/all_gather | solution.py:64
  45.5 1.5 fusion.126
  47.3 66.7 %all-gather.7.cloned.1.call-done = bf16[1024,3,2,128]{3,0,2,1:T(8,128)(2,1)} async-done(((bf16[64,3,2,128]{3,0,2,1:T(8,128)(2,1)}), bf16[1024,3,2,128]{3,0,2,1:T(8,128)(2,1)}) %all-gather.7.cloned.1.call-update) | async-done | bytes 1572880 | tf_op jit(solution)/shard_map/all_gather | solution.py:64
  113.9 1.4 fusion.125
  115.8 121.9 %all-gather.9.cloned.1.call-done = bf16[1024,3,2,128]{3,0,2,1:T(8,128)(2,1)} async-done(((bf16[16,3,2,128]{3,0,2,1:T(8,128)(2,1)}), bf16[1024,3,2,128]{3,0,2,1:T(8,128)(2,1)}) %all-gather.9.cloned.1.call-update) | async-done | bytes 1572880 | tf_op jit(solution)/shard_map/all_gather | solution.py:64
  237.7 1.4 fusion.124
  239.6 105.8 %all-gather.11.cloned.1.call-done = bf16[1024,3,2,128]{3,0,2,1:T(8,128)(2,1)} async-done(((bf16[8,3,2,128]{3,0,2,1:T(8,128)(2,1)}), bf16[1024,3,2,128]{3,0,2,1:T(8,128)(2,1)}) %all-gather.11.cloned.1.call-update) | async-done | bytes 1572880 | tf_op jit(solution)/shard_map/all_gather | solution.py:64
  345.4 1.4 fusion.123
  350.3 1.3 convolution_bitcast_fusion.3
  352.5 1.3 convolution_bitcast_fusion.5
  354.9 1.3 convolution_bitcast_fusion.7
  357.1 1.8 fusion.115
  358.9 6.9 psum.7
  368.2 1.4 select_reduce_fusion
  369.5 1.3 select_reduce_fusion.1
  370.8 9.5 all_gather.41
  381.7 1.3 pad_maximum_fusion.8
  383.0 1.3 copy.123
  385.0 5.1 all_gather.40
  392.1 1.3 pad_maximum_fusion.7
  393.3 1.4 copy.119
  396.2 1.3 pad_maximum_fusion.6
  397.5 1.4 copy.115
  399.8 34.2 %all_gather.43 = bf16[1024,2,128]{2,0,1:T(8,128)(2,1)} all-gather(bf16[64,2,128]{2,0,1:T(8,128)(2,1)S(1)} %select_reduce_fusion.2), channel_id=1, replica_groups=mesh['s4'=2,'s3'=4,'s2'=4,'s1'=4,'head'=4] {'s2','s1'}, dimensions={0}, use_global_device_ids=true | all-gather | bytes 557056 | tf_op jit(solution)/shard_map/all_gather | solution.py:154
  434.1 2.3 fusion.43
  438.1 115.1 %all_gather.45 = bf16[1024,2,128]{2,0,1:T(8,128)(2,1)S(1)} all-gather(bf16[16,2,128]{2,0,1:T(8,128)(2,1)} %select_reduce_fusion.1), channel_id=1, replica_groups=mesh['s4'=2,'s3'=4,'s2'=4,'s1'=4,'head'=4] {'s3','s2','s1'}, dimensions={0}, use_global_device_ids=true | all-gather | bytes 532480 | tf_op jit(solution)/shard_map/all_gather | solution.py:154
  553.3 2.2 fusion.57
  555.5 1.4 broadcast_in_dim.656
  556.9 1.8 copy.108
  558.7 226.1 %all_gather.47 = bf16[1024,2,128]{2,0,1:T(8,128)(2,1)} all-gather(bf16[8,2,128]{2,0,1:T(8,128)(2,1)} %select_reduce_fusion), channel_id=1, replica_groups=mesh['s4'=2,'s3'=4,'s2'=4,'s1'=4,'head'=4] {'s4','s3','s2','s1'}, dimensions={0}, use_global_device_ids=true | all-gather | bytes 528384 | tf_op jit(solution)/shard_map/all_gather | solution.py:154
  784.8 2.2 fusion.63
  787.0 1.4 broadcast_in_dim.658
  788.4 1.8 copy.110
  790.2 2.9 fusion.31
  793.1 1.7 copy.130
  794.7 30.1 %all_gather.42 = f32[1024,2,2]{2,1,0:T(2,128)S(1)} all-gather(f32[64,2,2]{2,1,0:T(2,128)} %copy.115), channel_id=1, replica_groups=mesh['s4'=2,'s3'=4,'s2'=4,'s1'=4,'head'=4] {'s2','s1'}, dimensions={0}, use_global_device_ids=true | all-gather | bytes 17408 | tf_op jit(solution)/shard_map/all_gather | solution.py:156
  826.1 1.4 fusion.6
  828.6 1.5 fusion.45
  830.9 115.6 %all_gather.44 = f32[1024,2,2]{2,1,0:T(2,128)S(1)} all-gather(f32[16,2,2]{2,1,0:T(2,128)S(1)} %copy-done.19), channel_id=1, replica_groups=mesh['s4'=2,'s3'=4,'s2'=4,'s1'=4,'head'=4] {'s3','s2','s1'}, dimensions={0}, use_global_device_ids=true | all-gather | bytes 16640 | tf_op jit(solution)/shard_map/all_gather | solution.py:156
  947.8 1.3 fusion.35
  950.1 1.4 fusion.59
  952.4 217.6 %all_gather.46 = f32[1024,2,2]{2,1,0:T(2,128)S(1)} all-gather(f32[8,2,2]{2,1,0:T(2,128)S(1)} %copy-done.21), channel_id=1, replica_groups=mesh['s4'=2,'s3'=4,'s2'=4,'s1'=4,'head'=4] {'s4','s3','s2','s1'}, dimensions={0}, use_global_device_ids=true | all-gather | bytes 16512 | tf_op jit(solution)/shard_map/all_gather | solution.py:156
  1171.3 1.3 fusion.50
  1173.7 1.4 fusion.61
  1176.0 1.8 subtract_exponential_fusion
  1179.0 2.1 fusion.30
  (223 shorter events, 38.4 us)
Async XLA Ops:
  7.2 5.2 copy-start.3
  7.2 5.2 copy-start.2
  7.2 5.2 copy-start.6
  7.2 3.0 copy-start.51
  7.2 38.3 %all-gather.5.cloned.1.call-start = ((), (), s32[]{:S(2)}) async-start(), calls=%async_computation | async-start | bytes 1966080 | tf_op jit(solution)/shard_map/all_gather | solution.py:64
  9.3 6.4 copy-start.16
  10.2 103.7 %all-gather.7.cloned.1.call-start = ((), (), s32[]{:S(2)}) async-start(), calls=%async_computation.1 | async-start | bytes 1671168 | tf_op jit(solution)/shard_map/all_gather | solution.py:64
  10.3 338.5 %copy-start.38 = (pred[4,2]{0,1:T(4,128)(4,1)}, pred[4,2]{0,1:T(4,128)(4,1)S(1)}, u32[]{:S(2)}) copy-start(pred[4,2]{0,1:T(4,128)(4,1)S(1)} %iota_compare_fusion.10) | copy-start | bytes 28
  12.2 225.5 %all-gather.9.cloned.1.call-start = ((), (), s32[]{:S(2)}) async-start(), calls=%async_computation.2 | async-start | bytes 1597440 | tf_op jit(solution)/shard_map/all_gather | solution.py:64
  12.4 337.1 %copy-start.39 = (pred[16,2]{0,1:T(4,128)(4,1)}, pred[16,2]{0,1:T(4,128)(4,1)S(1)}, u32[]{:S(2)}) copy-start(pred[16,2]{0,1:T(4,128)(4,1)S(1)} %iota_compare_fusion.9) | copy-start | bytes 100
  12.7 2.9 copy-start.24
  13.3 332.1 %all-gather.11.cloned.1.call-start = ((), (), s32[]{:S(2)}) async-start(), calls=%async_computation.3 | async-start | bytes 1585152 | tf_op jit(solution)/shard_map/all_gather | solution.py:64
  13.4 33.5 %copy-start.40 = (pred[32,2]{0,1:T(4,128)(4,1)}, pred[32,2]{0,1:T(4,128)(4,1)S(1)}, u32[]{:S(2)}) copy-start(pred[32,2]{0,1:T(4,128)(4,1)S(1)} %iota_compare_fusion.8) | copy-start | bytes 196
  13.6 1.9 copy-start.35
  14.4 332.7 %copy-start.26 = (pred[256,2]{0,1:T(4,128)(4,1)}, pred[256,2]{0,1:T(4,128)(4,1)S(1)}, u32[]{:S(2)}) copy-start(pred[256,2]{0,1:T(4,128)(4,1)S(1)} %broadcast_in_dim.619) | copy-start | bytes 1540
  15.3 331.7 %copy-start.29 = (pred[256,2]{0,1:T(4,128)(4,1)}, pred[256,2]{0,1:T(4,128)(4,1)S(1)}, u32[]{:S(2)}) copy-start(pred[256,2]{0,1:T(4,128)(4,1)S(1)} %broadcast_in_dim.611) | copy-start | bytes 1540
  15.8 331.4 %copy-start.31 = (pred[256,2]{0,1:T(4,128)(4,1)}, pred[256,2]{0,1:T(4,128)(4,1)S(1)}, u32[]{:S(2)}) copy-start(pred[256,2]{0,1:T(4,128)(4,1)S(1)} %broadcast_in_dim.602) | copy-start | bytes 1540
  239.1 113.5 %copy-start.7 = (f32[2,16,1024]{2,1,0:T(8,128)}, f32[2,16,1024]{2,1,0:T(8,128)S(1)}, u32[]{:S(2)}) copy-start(f32[2,16,1024]{2,1,0:T(8,128)S(1)} %get-tuple-element.59) | copy-start | bytes 393220
  346.7 8.1 copy-start.14
  346.9 3.3 copy-start.33
  349.1 2.6 copy-start.42
  350.3 2.3 copy-start.43
  350.3 4.4 copy-start.23
  350.3 4.4 copy-start.41
  351.6 3.1 copy-start.34
  352.5 4.5 copy-start.27
  354.9 2.2 copy-start.50
  357.0 8.8 copy-start.46
  366.0 3.6 copy-start.4
  399.8 34.3 %copy-start.15 = (bf16[64,2,128]{2,0,1:T(8,128)(2,1)}, bf16[64,2,128]{2,0,1:T(8,128)(2,1)S(1)}, u32[]{:S(2)}) copy-start(bf16[64,2,128]{2,0,1:T(8,128)(2,1)S(1)} %select_reduce_fusion.2) | copy-start | bytes 98308
  434.0 119.2 %copy-start.8 = (f32[2,16,1024]{2,1,0:T(8,128)S(1)}, f32[2,16,1024]{2,1,0:T(8,128)}, u32[]{:S(2)}) copy-start(f32[2,16,1024]{2,1,0:T(8,128)} %copy-done.7) | copy-start | bytes 393220
  556.9 233.3 %copy-start.5 = (bf16[256,2,128]{0,2,1:T(8,128)(2,1)S(1)}, bf16[256,2,128]{0,2,1:T(8,128)(2,1)}, u32[]{:S(2)}) copy-start(bf16[256,2,128]{0,2,1:T(8,128)(2,1)} %copy-done.4) | copy-start | bytes 393220
  824.8 1.2 copy-start.18
  824.8 1.2 copy-start.20
  825.7 1.8 copy-start
  826.0 2.5 copy-start.13
  827.7 3.2 copy-start.19
  949.3 3.2 copy-start.21
  1170.1 1.2 copy-start.36
  1170.1 1.2 copy-start.44
  1170.1 2.5 copy-start.1
  1172.6 3.4 copy-start.45
  1175.9 1.9 copy-start.9
  1175.9 1.9 copy-start.10
  1175.9 1.9 copy-start.11
  1175.9 1.9 copy-start.28
  1175.9 1.9 copy-start.30
  1176.0 1.9 copy-start.32
  (8 other events, 6.5 us)
Sparse Core Ops, SparseCore 0:
  10.3 35.1 all-gather.4
  49.4 64.4 all-gather.6
  116.6 121.0 all-gather.8
  242.8 102.5 all-gather.10
where the time goes:
time: 1190 us
  blocking collectives  760 us (64%)
  waiting for transfers between devices  321 us (27%)
  local copies, waits for them, and re-layouts  37.1 us (3%)
  matrix products  34.1 us (3%)
  other arithmetic  20.9 us (2%)
  between operations  14.5 us (1%)
    all_gather x4, blocking collectives, shards(): lax.all_gather(dout_sel, level['axes'], axis=0, tiled=True)  385 us
    all_gather x4, blocking collectives, shards(): lax.all_gather(stats, level['axes'], axis=0, tiled=True)  368 us
    all_gather x4, waiting for transfers between devices, shards(): gathered = lax.all_gather(packed, axes, axis=0, tiled=True)  321 us
  transfers between devices with their start and end apart: 4, of which 4 were waited for; matrix products, arithmetic and copies ran while one was open for 1% of the time, Pallas kernels for 0%

commit v1 on v0

--- a/solution.py
+++ b/solution.py
@@ -11,6 +11,18 @@
 RATES = (1, RATE2, RATE3, RATE4)
 neg_fill = -1e30
 epsilon = 1e-05
+
+
+def sums_all_point(inp, across):
+    return jnp.concatenate(
+        jax.lax.all_to_all(
+            jnp.stack([inp for _ in range(jax.lax.axis_size(across))], axis=0),
+            split_axis=0,
+            concat_axis=0,
+            axis_name=across,
+        ),
+        axis=0,
+    )
 
 
 def pick_rows(source, wanted, stride):
@@ -151,7 +163,7 @@
         query_grad = query_grad + put_rows(
             grad_sel * score_scale, level["wanted"], level["stride"], 0.0
         )
-        level["dout_all"] = lax.all_gather(dout_sel, level["axes"], axis=0, tiled=True)
+        level["dout_all"] = sums_all_point(dout_sel, level["axes"])
         stats = jnp.stack([level["lse_sel"], delta_sel], axis=1)
         level["stats_all"] = lax.all_gather(stats, level["axes"], axis=0, tiled=True)
     key_grad = jnp.zeros((tok_dev, heads_dev, head_size), jnp.float32)

time: 1190 us -> 884 us (0.74)
  blocking collectives: 760 us -> 391 us
  starting transfers between devices: 0.16 us -> 22.1 us
  waiting for transfers between devices: 321 us -> 342 us
  local copies, waits for them, and re-layouts: 37.1 us -> 52.5 us
    all_gather x4 -> x0, blocking collectives: 385 us -> none  [shards(): lax.all_gather(dout_sel, level['axes'], axis=0, tiled=True)]
    all_to_all x0 -> x4, waiting for transfers between devices: none -> 24.7 us  [sums_all_point(): jax.lax.all_to_all(jnp.stack([inp for _ in range(jax.lax.axis_size(across...]
    all_to_all x0 -> x4, starting transfers between devices: none -> 22 us  [sums_all_point(): jax.lax.all_to_all(jnp.stack([inp for _ in range(jax.lax.axis_size(across...]
    all_gather x4, blocking collectives: 368 us -> 384 us  [shards(): lax.all_gather(stats, level['axes'], axis=0, tiled=True)]
  transfers between devices with their start and end apart: 4 -> 8, of which waited for: 4 -> 6; matrix products, arithmetic and copies ran while one was open for 1% -> 8% of each run, Pallas kernels for 0% -> 0%
where the time goes in v1:
time: 884 us; the launch traced here: 882 us
  blocking collectives  391 us (44%)
  waiting for transfers between devices  342 us (39%)
  local copies, waits for them, and re-layouts  52.5 us (6%)
  matrix products  39 us (4%)
  starting transfers between devices  22.1 us (2%)
  other arithmetic  20.2 us (2%)
  between operations  14.6 us (2%)
    all_gather x4, blocking collectives, shards(): lax.all_gather(stats, level['axes'], axis=0, tiled=True)  384 us
    all_gather x4, waiting for transfers between devices, shards(): gathered = lax.all_gather(packed, axes, axis=0, tiled=True)  317 us
    all_to_all x4, waiting for transfers between devices, sums_all_point(): jax.lax.all_to_all(jnp.stack([inp for _ in range(jax.lax.axis_size(across...  24.7 us
    broadcast_in_dim x45, local copies, waits for them, and re-layouts, put_rows(): jnp.where(column == target, compact[:, None], jnp.asarray(filler, compact...  24.6 us
    all_to_all x4, starting transfers between devices, sums_all_point(): jax.lax.all_to_all(jnp.stack([inp for _ in range(jax.lax.axis_size(across...  22 us
  transfers between devices with their start and end apart: 8, of which 6 were waited for; matrix products, arithmetic and copies ran while one was open for 8% of the time, Pallas kernels for 0%

profile of v1, /device:TPU:9, one launch (start us, length us, event | category | flops | bytes accessed | tf_op | source)
XLA Modules:
  0.0 881.9 jit_solution(7838742846553844626)
XLA Ops:
  21.4 24.0 %all-gather.5.cloned.1.call-done = bf16[1024,3,2,128]{3,0,2,1:T(8,128)(2,1)} async-done(((bf16[256,3,2,128]{3,0,2,1:T(8,128)(2,1)}), bf16[1024,3,2,128]{3,0,2,1:T(8,128)(2,1)}) %all-gather.5.cloned.1.call-update) | async-done | bytes 1572880 | tf_op jit(solution)/shard_map/all_gather | solution.py:76
  45.4 1.5 fusion.132
  47.9 66.0 %all-gather.7.cloned.1.call-done = bf16[1024,3,2,128]{3,0,2,1:T(8,128)(2,1)} async-done(((bf16[64,3,2,128]{3,0,2,1:T(8,128)(2,1)}), bf16[1024,3,2,128]{3,0,2,1:T(8,128)(2,1)}) %all-gather.7.cloned.1.call-update) | async-done | bytes 1572880 | tf_op jit(solution)/shard_map/all_gather | solution.py:76
  113.9 1.4 fusion.131
  115.8 121.9 %all-gather.9.cloned.1.call-done = bf16[1024,3,2,128]{3,0,2,1:T(8,128)(2,1)} async-done(((bf16[16,3,2,128]{3,0,2,1:T(8,128)(2,1)}), bf16[1024,3,2,128]{3,0,2,1:T(8,128)(2,1)}) %all-gather.9.cloned.1.call-update) | async-done | bytes 1572880 | tf_op jit(solution)/shard_map/all_gather | solution.py:76
  239.6 105.2 %all-gather.11.cloned.1.call-done = bf16[1024,3,2,128]{3,0,2,1:T(8,128)(2,1)} async-done(((bf16[8,3,2,128]{3,0,2,1:T(8,128)(2,1)}), bf16[1024,3,2,128]{3,0,2,1:T(8,128)(2,1)}) %all-gather.11.cloned.1.call-update) | async-done | bytes 1572880 | tf_op jit(solution)/shard_map/all_gather | solution.py:76
  355.9 1.8 fusion.121
  357.7 6.9 psum.7
  365.9 1.4 select_reduce_fusion.1
  372.0 1.4 select_reduce_fusion.2
  374.3 5.7 all-to-all-start
  380.0 2.2 fusion.63
  382.2 2.2 fusion.57
  384.5 2.3 fusion.43
  386.8 37.1 %all_gather.29 = f32[1024,2,2]{2,1,0:T(2,128)S(1)} all-gather(f32[64,2,2]{2,1,0:T(2,128)} %copy.115), channel_id=1, replica_groups=mesh['s4'=2,'s3'=4,'s2'=4,'s1'=4,'head'=4] {'s2','s1'}, dimensions={0}, use_global_device_ids=true | all-gather | bytes 17408 | tf_op jit(solution)/shard_map/all_gather | solution.py:168
  425.1 1.8 fusion.123
  427.9 3.5 all-to-all-start.1
  435.2 1.6 broadcast_in_dim.654
  436.8 1.8 copy.106
  438.6 1.4 broadcast_in_dim.656
  440.0 1.8 copy.108
  441.8 1.4 broadcast_in_dim.658
  443.2 1.8 copy.110
  445.1 1.8 copy.116
  446.9 125.7 %all_gather.30 = f32[1024,2,2]{2,1,0:T(2,128)S(1)} all-gather(f32[16,2,2]{2,1,0:T(2,128)} %copy.120), channel_id=1, replica_groups=mesh['s4'=2,'s3'=4,'s2'=4,'s1'=4,'head'=4] {'s3','s2','s1'}, dimensions={0}, use_global_device_ids=true | all-gather | bytes 16640 | tf_op jit(solution)/shard_map/all_gather | solution.py:168
  572.6 1.6 fusion.124
  574.9 216.6 %all_gather.31 = f32[1024,2,2]{2,1,0:T(2,128)S(1)} all-gather(f32[8,2,2]{2,1,0:T(2,128)} %copy.125), channel_id=1, replica_groups=mesh['s4'=2,'s3'=4,'s2'=4,'s1'=4,'head'=4] {'s4','s3','s2','s1'}, dimensions={0}, use_global_device_ids=true | all-gather | bytes 16512 | tf_op jit(solution)/shard_map/all_gather | solution.py:168
  791.5 1.6 fusion.125
  794.0 5.1 all_gather.28
  799.1 2.0 fusion.35
  801.1 1.6 stack.91
  802.6 5.1 all-to-all-start.2
  808.3 1.4 fusion.6
  809.7 3.1 subtract_exponential_fusion
  812.8 2.2 fusion.31
  815.0 13.9 %all-to-all-done.2 = bf16[64,16,2,128]{3,1,2,0:T(8,128)(2,1)} async-done(((bf16[64,16,2,128]{3,1,2,0:T(8,128)(2,1)}), bf16[64,16,2,128]{3,1,2,0:T(8,128)(2,1)}, u32[]{:S(2)}, u32[]{:S(2)}) %all-to-all-start.2) | async-done | bytes 524320 | tf_op jit(solution)/shard_map/all_to_all | solution.py:18
  828.9 1.5 stack.95
  830.5 7.7 all-to-all-start.3
  838.2 1.9 fusion.50
  843.7 1.5 fusion.45
  847.6 1.4 fusion.59
  849.9 10.8 %all-to-all-done.3 = bf16[128,8,2,128]{3,1,2,0:T(8,128)(2,1)} async-done(((bf16[128,8,2,128]{3,1,2,0:T(8,128)(2,1)}), bf16[128,8,2,128]{3,1,2,0:T(8,128)(2,1)}, u32[]{:S(2)}, u32[]{:S(2)}) %all-to-all-start.3) | async-done | bytes 524320 | tf_op jit(solution)/shard_map/all_to_all | solution.py:18
  863.8 2.2 fusion.61
  866.0 1.4 broadcast_in_dim.672
  867.4 1.8 copy.129
  869.2 1.7 fusion.29
  870.9 1.7 copy.136
  872.6 2.0 fusion.30
  (256 shorter events, 53.8 us)
Async XLA Ops:
  7.2 4.6 copy-start.9
  7.2 4.6 copy-start.5
  7.2 4.5 copy-start.10
  7.2 38.2 %all-gather.5.cloned.1.call-start = ((), (), s32[]{:S(2)}) async-start(), calls=%async_computation.4 | async-start | bytes 1966080 | tf_op jit(solution)/shard_map/all_gather | solution.py:76
  9.3 9.3 %copy-start.17 = (bf16[256,2,128]{2,1,0:T(2,128)(2,1)S(1)}, bf16[256,2,128]{2,1,0:T(2,128)(2,1)}, u32[]{:S(2)}) copy-start(bf16[256,2,128]{2,1,0:T(2,128)(2,1)} %param.9) | copy-start | bytes 393220
  10.2 103.7 %all-gather.7.cloned.1.call-start = ((), (), s32[]{:S(2)}) async-start(), calls=%async_computation.5 | async-start | bytes 1671168 | tf_op jit(solution)/shard_map/all_gather | solution.py:76
  10.3 9.2 %copy-start.43 = (pred[4,2]{0,1:T(4,128)(4,1)}, pred[4,2]{0,1:T(4,128)(4,1)S(1)}, u32[]{:S(2)}) copy-start(pred[4,2]{0,1:T(4,128)(4,1)S(1)} %iota_compare_fusion.10) | copy-start | bytes 28
  10.9 10.5 %copy-start.13 = (bf16[64,2,128]{2,0,1:T(8,128)(2,1)}, bf16[64,2,128]{2,0,1:T(8,128)(2,1)S(1)}, u32[]{:S(2)}) copy-start(bf16[64,2,128]{2,0,1:T(8,128)(2,1)S(1)} %get-tuple-element.17) | copy-start | bytes 98308
  10.9 10.5 %copy-start.18 = (bf16[64,2,128]{2,0,1:T(8,128)(2,1)}, bf16[64,2,128]{2,0,1:T(8,128)(2,1)S(1)}, u32[]{:S(2)}) copy-start(bf16[64,2,128]{2,0,1:T(8,128)(2,1)S(1)} %get-tuple-element.16) | copy-start | bytes 98308
  11.6 226.1 %all-gather.9.cloned.1.call-start = ((), (), s32[]{:S(2)}) async-start(), calls=%async_computation.6 | async-start | bytes 1597440 | tf_op jit(solution)/shard_map/all_gather | solution.py:76
  11.7 6.1 copy-start.45
  12.7 332.1 %all-gather.11.cloned.1.call-start = ((), (), s32[]{:S(2)}) async-start(), calls=%async_computation.7 | async-start | bytes 1585152 | tf_op jit(solution)/shard_map/all_gather | solution.py:76
  12.8 6.7 copy-start.47
  13.0 4.9 copy-start.40
  47.8 298.7 %copy-start.24 = (pred[256,2]{0,1:T(4,128)(4,1)S(1)}, pred[256,2]{0,1:T(4,128)(4,1)}, u32[]{:S(2)}) copy-start(pred[256,2]{0,1:T(4,128)(4,1)} %broadcast_in_dim.619) | copy-start | bytes 1540
  47.8 298.7 %copy-start.28 = (pred[256,2]{0,1:T(4,128)(4,1)S(1)}, pred[256,2]{0,1:T(4,128)(4,1)}, u32[]{:S(2)}) copy-start(pred[256,2]{0,1:T(4,128)(4,1)} %broadcast_in_dim.611) | copy-start | bytes 1540
  47.8 298.7 %copy-start.31 = (pred[256,2]{0,1:T(4,128)(4,1)S(1)}, pred[256,2]{0,1:T(4,128)(4,1)}, u32[]{:S(2)}) copy-start(pred[256,2]{0,1:T(4,128)(4,1)} %broadcast_in_dim.602) | copy-start | bytes 1540
  47.8 298.7 %copy-start.55 = (f32[2,256]{1,0:T(2,128)S(1)}, f32[2,256]{1,0:T(2,128)}, u32[]{:S(2)}) copy-start(f32[2,256]{1,0:T(2,128)} %copy-done.54) | copy-start | bytes 6148
  47.9 299.8 %copy-start.19 = (pred[64,4,2]{1,0,2:T(8,128)(4,1)S(1)}, pred[64,4,2]{1,0,2:T(8,128)(4,1)}, u32[]{:S(2)}) copy-start(pred[64,4,2]{1,0,2:T(8,128)(4,1)} %broadcast_in_dim.628) | copy-start | bytes 1540
  47.9 299.8 %copy-start.20 = (pred[64,4,2]{1,0,2:T(8,128)(4,1)S(1)}, pred[64,4,2]{1,0,2:T(8,128)(4,1)}, u32[]{:S(2)}) copy-start(pred[64,4,2]{1,0,2:T(8,128)(4,1)} %broadcast_in_dim.632) | copy-start | bytes 1540
  47.9 299.8 %copy-start.44 = (pred[4,2]{0,1:T(4,128)(4,1)S(1)}, pred[4,2]{0,1:T(4,128)(4,1)}, u32[]{:S(2)}) copy-start(pred[4,2]{0,1:T(4,128)(4,1)} %copy-done.43) | copy-start | bytes 28
  115.3 232.9 %copy-start.42 = (pred[16,16,2]{1,0,2:T(8,128)(4,1)S(1)}, pred[16,16,2]{1,0,2:T(8,128)(4,1)}, u32[]{:S(2)}) copy-start(pred[16,16,2]{1,0,2:T(8,128)(4,1)} %broadcast_in_dim.642) | copy-start | bytes 1540
  115.3 232.9 %copy-start.46 = (pred[16,2]{0,1:T(4,128)(4,1)S(1)}, pred[16,2]{0,1:T(4,128)(4,1)}, u32[]{:S(2)}) copy-start(pred[16,2]{0,1:T(4,128)(4,1)} %copy-done.45) | copy-start | bytes 100
  239.1 118.6 %copy-start.11 = (f32[2,16,1024]{2,1,0:T(8,128)}, f32[2,16,1024]{2,1,0:T(8,128)S(1)}, u32[]{:S(2)}) copy-start(f32[2,16,1024]{2,1,0:T(8,128)S(1)} %get-tuple-element.59) | copy-start | bytes 393220
  346.1 7.5 copy-start.15
  355.9 8.8 copy-start.57
  365.9 16.3 %copy-start.37 = (bf16[8,2,128]{2,0,1:T(8,128)(2,1)}, bf16[8,2,128]{2,0,1:T(8,128)(2,1)S(1)}, u32[]{:S(2)}) copy-start(bf16[8,2,128]{2,0,1:T(8,128)(2,1)S(1)} %select_reduce_fusion) | copy-start | bytes 12292
  374.3 52.5 %all-to-all-start = ((bf16[4,256,2,128]{1,3,2,0:T(8,128)(2,1)}), bf16[4,256,2,128]{1,3,2,0:T(8,128)(2,1)S(1)}, u32[]{:S(2)}, u32[]{:S(2)}) async-start(bf16[4,256,2,128]{1,3,2,0:T(8,128)(2,1)} %stack.83), calls=%async_computation | async-start | bytes 1048576 | tf_op jit(solution)/shard_map/all_to_all | solution.py:18
  384.5 39.4 %copy-start.59 = (f32[8,2]{0,1:T(2,128)S(1)}, f32[8,2]{0,1:T(2,128)}, u32[]{:S(2)}) copy-start(f32[8,2]{0,1:T(2,128)} %select_reduce_fusion.14) | copy-start | bytes 196
  386.8 40.1 %copy-start.16 = (bf16[64,2,128]{2,0,1:T(8,128)(2,1)S(1)}, bf16[64,2,128]{2,0,1:T(8,128)(2,1)}, u32[]{:S(2)}) copy-start(bf16[64,2,128]{2,0,1:T(8,128)(2,1)} %select_reduce_fusion.2) | copy-start | bytes 98308
  425.1 6.4 copy-start.50
  426.9 15.0 %copy-start.1 = (bf16[4,256,2,128]{1,3,2,0:T(8,128)(2,1)}, bf16[4,256,2,128]{1,3,2,0:T(8,128)(2,1)S(1)}, u32[]{:S(2)}) copy-start(bf16[4,256,2,128]{1,3,2,0:T(8,128)(2,1)S(1)} %all-to-all-done) | copy-start | bytes 1572868
  427.9 373.2 %all-to-all-start.1 = ((bf16[16,64,2,128]{3,1,2,0:T(8,128)(2,1)}), bf16[16,64,2,128]{3,1,2,0:T(8,128)(2,1)S(1)}, u32[]{:S(2)}, u32[]{:S(2)}) async-start(bf16[16,64,2,128]{3,1,2,0:T(8,128)(2,1)} %stack.87), calls=%async_computation.1 | async-start | bytes 1048576 | tf_op jit(solution)/shard_map/all_to_all | solution.py:18
  801.1 11.7 %copy-start.3 = (bf16[16,64,2,128]{3,1,2,0:T(8,128)(2,1)}, bf16[16,64,2,128]{3,1,2,0:T(8,128)(2,1)S(1)}, u32[]{:S(2)}) copy-start(bf16[16,64,2,128]{3,1,2,0:T(8,128)(2,1)S(1)} %all-to-all-done.1) | copy-start | bytes 1572868
  802.6 26.3 %all-to-all-start.2 = ((bf16[64,16,2,128]{3,1,2,0:T(8,128)(2,1)}), bf16[64,16,2,128]{3,1,2,0:T(8,128)(2,1)}, u32[]{:S(2)}, u32[]{:S(2)}) async-start(bf16[64,16,2,128]{3,1,2,0:T(8,128)(2,1)} %stack.91), calls=%async_computation.2 | async-start | bytes 1048576 | tf_op jit(solution)/shard_map/all_to_all | solution.py:18
  815.0 23.2 %copy-start.41 = (bf16[8,2,128]{2,0,1:T(8,128)(2,1)S(1)}, bf16[8,2,128]{2,0,1:T(8,128)(2,1)}, u32[]{:S(2)}) copy-start(bf16[8,2,128]{2,0,1:T(8,128)(2,1)} %copy-done.40) | copy-start | bytes 12292
  815.0 23.2 %copy-start.52 = (f32[2,1024]{1,0:T(2,128)S(1)}, f32[2,1024]{1,0:T(2,128)}, u32[]{:S(2)}) copy-start(f32[2,1024]{1,0:T(2,128)} %copy.126) | copy-start | bytes 24580
  815.0 23.2 %copy-start.53 = (pred[1024,8]{0,1:T(8,128)(4,1)S(1)}, pred[1024,8]{0,1:T(8,128)(4,1)}, u32[]{:S(2)}) copy-start(pred[1024,8]{0,1:T(8,128)(4,1)} %iota_compare_fusion.6) | copy-start | bytes 24580
  815.0 25.9 %copy-start.6 = (f32[1024,1,2]{2,1,0:T(1,128)S(1)}, f32[1024,1,2]{2,1,0:T(1,128)}, u32[]{:S(2)}) copy-start(f32[1024,1,2]{2,1,0:T(1,128)} %get-tuple-element.29) | copy-start | bytes 24580
  815.0 26.7 %copy-start.7 = (f32[1024,1,2]{2,1,0:T(1,128)S(1)}, f32[1024,1,2]{2,1,0:T(1,128)}, u32[]{:S(2)}) copy-start(f32[1024,1,2]{2,1,0:T(1,128)} %get-tuple-element.31) | copy-start | bytes 24580
  830.5 11.4 %copy-start.8 = (f32[1024,1,2]{2,1,0:T(1,128)S(1)}, f32[1024,1,2]{2,1,0:T(1,128)}, u32[]{:S(2)}) copy-start(f32[1024,1,2]{2,1,0:T(1,128)} %get-tuple-element.33) | copy-start | bytes 24580
  830.5 12.2 %copy-start.2 = (bf16[4,256,2,128]{1,3,2,0:T(8,128)(2,1)S(1)}, bf16[4,256,2,128]{1,3,2,0:T(8,128)(2,1)}, u32[]{:S(2)}) copy-start(bf16[4,256,2,128]{1,3,2,0:T(8,128)(2,1)} %copy-done.1) | copy-start | bytes 1572868
  830.5 30.3 %all-to-all-start.3 = ((bf16[128,8,2,128]{3,1,2,0:T(8,128)(2,1)}), bf16[128,8,2,128]{3,1,2,0:T(8,128)(2,1)}, u32[]{:S(2)}, u32[]{:S(2)}) async-start(bf16[128,8,2,128]{3,1,2,0:T(8,128)(2,1)} %stack.95), calls=%async_computation.3 | async-start | bytes 1048576 | tf_op jit(solution)/shard_map/all_to_all | solution.py:18
  847.4 13.3 %copy-start.62 = (f32[2,1024,8]{1,2,0:T(8,128)S(1)}, f32[2,1024,8]{1,2,0:T(8,128)}, u32[]{:S(2)}) copy-start(f32[2,1024,8]{1,2,0:T(8,128)} %fusion.50) | copy-start | bytes 196612
  849.0 14.8 %copy-start.39 = (bf16[8,2,128]{2,0,1:T(8,128)(2,1)S(1)}, bf16[8,2,128]{2,0,1:T(8,128)(2,1)}, u32[]{:S(2)}) copy-start(bf16[8,2,128]{2,0,1:T(8,128)(2,1)} %copy-done.38) | copy-start | bytes 12292
  862.0 7.2 copy-start
  862.0 7.2 copy-start.27
  862.0 7.2 copy-start.30
  (23 other events, 67.3 us)
Sparse Core Ops, SparseCore 0:
  10.3 35.1 all-gather.4
  49.4 64.4 all-gather.6
  116.5 121.0 all-gather.8
  242.2 102.5 all-gather.10
